TPU v7x, 32 devices: a whole 2x2x4 slice. The times are simulated.
32 devices in a mesh: groups: 2 (over y), brick: 4 (over z), split: 2 (over x), sub: 2 (over core).
Axes of the slice: x: 2, y: 2, z: 4, core: 2. Of those that a mesh axis runs over, the one named last changes fastest.
Arguments:
- grad_out: bfloat16 [128, 32, 512], P(('groups', 'brick', 'split', 'sub')), parts along dimension 0, may hold values from -6 to 6
- features: bfloat16 [128, 32, 512], P(('groups', 'brick', 'split', 'sub')), parts along dimension 0, may hold values from -6 to 6
- kernel: bfloat16 [27, 32, 32], replicated, may hold values from -0.21875 to 0.21875
- block_count: int32 [32], P(('groups', 'brick', 'split', 'sub')), parts along dimension 0, may hold values from 1 to 4, as said below
- neighbours: int32 [128, 26], P(('groups', 'brick', 'split', 'sub')), parts along dimension 0, may hold values from 0 to 16, as said below
Outputs:
- grad_features: bfloat16 [128, 32, 512], P(('groups', 'brick', 'split', 'sub')), parts along dimension 0
- kernel_grad: float32 [54, 32, 32], P('groups'), parts along dimension 0
There are 2 independent parts, one for each index of `groups`. A program takes and returns all parts, laid end to end along the dimension named above; an argument that names none is the same for every part. Nothing has to cross between parts.
Inputs may be any that keep to these rules, and one draw needn't show every extreme that they name: `block_count`: in every brick one device holds exactly 4 live blocks. `neighbours`: entry (q, k) is the slot, within the brick at block height offset c of direction k (periodic), of the active block at the neighbouring position (periodic in the first two dimensions), or 16 if that position is inactive; rows of slots that are not live hold 16; every active block has one slot.
All inputs are finite; a program needn't handle non-finite values.
Results may differ from a plain program's by a relative error of at most 0.001.
Values may be sent and summed in bfloat16 or wider, within the bound.
No kernel may reach another device: no remote copies, remote signals or barrier semaphores. Data moves between devices by JAX's collectives and lax.ppermute only.
A program may use at most 64 MiB of HBM per device.

v0:
```python
import math
import jax
import jax.numpy as jnp
from jax import lax
from jax.sharding import PartitionSpec as P

DIRECTIONS = [(a, b, c) for a in (-1, 0, 1) for b in (-1, 0, 1) for c in (-1, 0, 1)]
NEIGHBOURS = [d for d in DIRECTIONS if d != (0, 0, 0)]


def from_behind(block, axis, distance):
    devices = range(lax.axis_size(axis))
    route = [((i - distance) % len(devices), i) for i in devices]
    return lax.ppermute(block, axis, route)


def window(offset):
    if offset < 0:
        return slice(7, 8)
    if offset > 0:
        return slice(0, 1)
    return slice(0, 8)


def assemble(pieces):
    planes = []
    for a in (-1, 0, 1):
        row_list = []
        for b in (-1, 0, 1):
            row_list.append(jnp.concatenate([pieces[a, b, c] for c in (-1, 0, 1)], axis=4))
        planes.append(jnp.concatenate(row_list, axis=3))
    return jnp.concatenate(planes, axis=2)


def contract(padded, source, kernel):
    blocks_here, channels = (source.shape[0], source.shape[1])
    input_grad = jnp.zeros((blocks_here, channels, 512), jnp.float32)
    weight_grads = {}
    for c in (-1, 0, 1):
        shifted = jnp.concatenate(
            [
                padded[:, :, 1 - a : 9 - a, 1 - b : 9 - b, 1 - c : 9 - c].reshape(
                    blocks_here, channels, 512
                )
                for a in (-1, 0, 1)
                for b in (-1, 0, 1)
            ],
            axis=1,
        )
        offset_ids = [(a + 1) * 9 + (b + 1) * 3 + (c + 1) for a in (-1, 0, 1) for b in (-1, 0, 1)]
        stacked = jnp.stack([kernel[i] for i in offset_ids], axis=0)
        mixing = jnp.transpose(stacked, (1, 0, 2)).reshape(channels, 9 * channels)
        input_grad = input_grad + jnp.einsum(
            "ik,bkv->biv", mixing, shifted, preferred_element_type=jnp.float32
        )
        weight_part = jnp.einsum(
            "biv,bkv->ik", source, shifted, preferred_element_type=jnp.float32
        ).reshape(channels, 9, channels)
        for j, i in enumerate(offset_ids):
            weight_grads[i] = weight_part[:, j]
    return (input_grad, jnp.stack([weight_grads[i] for i in range(27)], axis=0))


def with_zero(fetched_rows):
    return jnp.concatenate(
        [fetched_rows, jnp.zeros((1,) + fetched_rows.shape[1:], fetched_rows.dtype)], axis=0
    )


def on_device(grad_out, features, kernel, block_count, neighbours):
    blocks_here, channels = (grad_out.shape[0], grad_out.shape[1])
    cubes_here = grad_out.reshape(blocks_here, channels, 8, 8, 8)
    shell_rows = jnp.concatenate(
        [cubes_here[:, :, 0], cubes_here[:, :, 7], cubes_here[:, :, :, 0], cubes_here[:, :, :, 7]],
        axis=2,
    ).reshape(blocks_here, channels, 256)
    lower_layer = cubes_here[:, :, :, :, 0].reshape(blocks_here, channels * 64)
    upper_layer = cubes_here[:, :, :, :, 7].reshape(blocks_here, channels * 64)
    shell_all, lower_all, upper_all = (
        lax.all_gather(shell_rows, ("split", "sub"), axis=0, tiled=True),
        lax.all_gather(lower_layer, ("split", "sub"), axis=0, tiled=True),
        lax.all_gather(upper_layer, ("split", "sub"), axis=0, tiled=True),
    )
    from_below = from_behind(upper_all, "brick", 1)
    from_above = from_behind(lower_all, "brick", -1)
    shell_table = with_zero(shell_all)
    layer_tables = {-1: with_zero(from_below), 1: with_zero(from_above)}
    pieces = {(0, 0, 0): cubes_here}
    for k, (a, b, c) in enumerate(NEIGHBOURS):
        slot_index = neighbours[:, k]
        if c == 0:
            fetched = jnp.take(shell_table, slot_index, axis=0).reshape(
                blocks_here, channels, 4, 8, 8
            )
            if a != 0:
                face_rows = fetched[:, :, 1 if a < 0 else 0]
                pieces[a, b, c] = face_rows[:, :, None, window(b), :]
            else:
                face_rows = fetched[:, :, 3 if b < 0 else 2]
                pieces[a, b, c] = face_rows[:, :, :, None, :]
        else:
            layer_rows = jnp.take(layer_tables[c], slot_index, axis=0).reshape(
                blocks_here, channels, 8, 8
            )
            pieces[a, b, c] = layer_rows[:, :, window(a), window(b)][:, :, :, :, None]
    padded = assemble(pieces)
    live_mask = (jnp.arange(blocks_here) < block_count[0])[:, None, None]
    masked = jnp.where(live_mask, features, jnp.zeros_like(features))
    input_grad, weight_grads = contract(padded, masked, kernel)
    grad_features = jnp.where(live_mask, input_grad, jnp.zeros_like(input_grad)).astype(
        jnp.bfloat16
    )
    totals = lax.psum(weight_grads, ("brick", "split", "sub"))
    scaling = 1.0 / math.sqrt(
        lax.axis_size("brick") * lax.axis_size("split") * lax.axis_size("sub") * blocks_here * 512
    )
    return (grad_features, totals * scaling)


def solution(mesh):
    placed = (
        P(("groups", "brick", "split", "sub"), None, None),
        P(("groups", "brick", "split", "sub"), None, None),
        P(),
        P(("groups", "brick", "split", "sub")),
        P(("groups", "brick", "split", "sub"), None),
    )
    return jax.shard_map(
        on_device,
        mesh=mesh,
        in_specs=placed,
        out_specs=(P(("groups", "brick", "split", "sub"), None, None), P("groups", None, None)),
        check_vma=False,
    )
```

profile of v0, /device:TPU:0, one launch (start us, length us, event | category | flops | bytes accessed | tf_op | source)
XLA Modules:
  0.0 252.1 jit_solution(10741603956274095577)
XLA Ops:
  9.1 6.2 %all-gather = bf16[4,4,2048]{2,1,0:T(4,128)(2,1)S(1)} all-gather(bf16[1,4,2048]{2,1,0:T(4,128)(2,1)S(1)} %reshape.484), channel_id=1, replica_groups=mesh['groups'=2,'brick'=4,'split'=2,'sub'=2] {'split','sub'}, dimensions={0}, use_global_device_ids=true | all-gather | bytes 81920 | tf_op jit(solution)/shard_map/all_gather | solution.py:82
  15.3 2.2 collective-permute-start
  18.0 5.2 %all-gather.1 = bf16[4,4,2048]{2,1,0:T(4,128)(2,1)S(1)} all-gather(bf16[1,4,2048]{2,1,0:T(4,128)(2,1)S(1)} %reshape.486), channel_id=1, replica_groups=mesh['groups'=2,'brick'=4,'split'=2,'sub'=2] {'split','sub'}, dimensions={0}, use_global_device_ids=true | all-gather | bytes 81920 | tf_op jit(solution)/shard_map/all_gather | solution.py:81
  23.2 2.1 collective-permute-start.1
  36.5 6.1 %all_gather.10 = bf16[16,32,256]{2,1,0:T(8,128)(2,1)S(1)} all-gather(bf16[4,32,256]{2,1,0:T(8,128)(2,1)S(1)} %copy.281), channel_id=1, replica_groups=mesh['groups'=2,'brick'=4,'split'=2,'sub'=2] {'split','sub'}, dimensions={0}, use_global_device_ids=true | all-gather | bytes 327680 | tf_op jit(solution)/shard_map/all_gather | solution.py:80
  89.7 1.9 copy.344
  94.3 1.9 copy.342
  97.3 3.7 %maximum_maximum_fusion = bf16[4,32,9,10,10]{1,4,3,2,0:T(8,128)(2,1)S(1)} fusion(bf16[4,32,1,1,1]{1,4,3,2,0:T(2,128)(2,1)S(1)} %copy-done.33, bf16[4,32,1,1,8]{1,4,3,2,0:T(8,128)(2,1)S(1)} %copy-done.28, bf16[4,32,1,1,1]{1,4,3,2,0:T(2,128)(2,1)S(1)} %copy-done.31, bf16[4,32,1,8,1]{1,4,3,2,0:T(2,128)(2,1)S(1)} %copy-done.26, ...), kind=kLoop, calls=%fused_computation.26 | loop fusion | flops 4147200 | bytes 460800 | tf_op jit(solution)/shard_map/concatenate | solution.py:32
  101.0 2.2 fusion.7
  103.3 1.9 copy.341
  105.1 1.9 copy.340
  107.0 1.9 copy.339
  108.9 1.9 copy.330
  110.7 1.9 copy.329
  122.3 3.3 %maximum_maximum_fusion.1 = bf16[4,32,9,10,10]{1,4,3,2,0:T(8,128)(2,1)S(1)} fusion(bf16[4,32,8,1,1]{1,4,3,2,0:T(2,128)(2,1)} %copy-done.25, bf16[4,32,8,1,8]{1,4,3,2,0:T(8,128)(2,1)S(1)} %slice_bitcast_fusion.4, bf16[4,32,8,1,1]{1,4,3,2,0:T(2,128)(2,1)} %copy-done.23, bf16[4,32,8,8,1]{1,4,3,2,0:T(2,128)(2,1)S(1)} %copy.288, ...), kind=kLoop, calls=%fused_computation.27 | loop fusion | flops 4147200 | bytes 460800 | tf_op jit(solution)/shard_map/concatenate | solution.py:32
  125.5 2.5 fusion.6
  128.0 1.9 copy.347
  129.9 1.9 copy.346
  131.8 1.9 copy.345
  133.6 1.9 copy.335
  135.5 1.9 copy.334
  137.4 1.9 copy.333
  139.3 1.9 copy.325
  155.9 87.3 %all-reduce.5.cloned.1.call-done = f32[27,32,32]{1,2,0:T(8,128)} async-done(((f32[27,32,32]{1,2,0:T(8,128)}), f32[27,32,32]{1,2,0:T(8,128)}) %all-reduce.5.cloned.1.call-update) | async-done | bytes 110608 | tf_op jit(solution)/shard_map/psum | solution.py:113
  (364 shorter events, 88.7 us)
Async XLA Ops:
  7.2 18.1 %copy-start = (s32[4,26]{1,0:T(4,128)S(1)}, s32[4,26]{1,0:T(4,128)}, u32[]{:S(2)}) copy-start(s32[4,26]{1,0:T(4,128)} %param.13) | copy-start | bytes 1252
  7.2 236.1 %all-reduce.5.cloned.1.call-start = ((), (), s32[]{:S(2)}) async-start(), calls=%async_computation | async-start | bytes 884736 | tf_op jit(solution)/shard_map/psum | solution.py:113
  15.3 37.6 %collective-permute-start = (bf16[16,2048]{1,0:T(8,128)(2,1)S(1)}, bf16[16,2048]{1,0:T(8,128)(2,1)S(1)}, u32[]{:S(2)}, u32[]{:S(2)}) collective-permute-start(bf16[16,2048]{1,0:T(8,128)(2,1)S(1)} %reshape.485), channel_id=1, source_target_pairs={{12,0},{0,4},{4,8},{8,12},{13,1},{1,5},{5,9},{9,13},{14,2},{2,6},{... | collective-permute-start | bytes 196616 | tf_op jit(solution)/shard_map/ppermute | solution.py:14
  23.2 45.5 %collective-permute-start.1 = (bf16[16,2048]{1,0:T(8,128)(2,1)S(1)}, bf16[16,2048]{1,0:T(8,128)(2,1)S(1)}, u32[]{:S(2)}, u32[]{:S(2)}) collective-permute-start(bf16[16,2048]{1,0:T(8,128)(2,1)S(1)} %reshape.487), channel_id=1, source_target_pairs={{4,0},{8,4},{12,8},{0,12},{5,1},{9,5},{13,9},{1,13},{6,2},{10,6},{... | collective-permute-start | bytes 196616 | tf_op jit(solution)/shard_map/ppermute | solution.py:14
  60.5 36.8 %copy-start.23 = (bf16[4,32,8,1,1]{1,4,3,2,0:T(2,128)(2,1)}, bf16[4,32,8,1,1]{1,4,3,2,0:T(2,128)(2,1)S(1)}, u32[]{:S(2)}) copy-start(bf16[4,32,8,1,1]{1,4,3,2,0:T(2,128)(2,1)S(1)} %copy.292) | copy-start | bytes 6148
  75.5 21.8 %copy-start.24 = (bf16[4,32,8,1,1]{1,4,3,2,0:T(2,128)(2,1)}, bf16[4,32,8,1,1]{1,4,3,2,0:T(2,128)(2,1)S(1)}, u32[]{:S(2)}) copy-start(bf16[4,32,8,1,1]{1,4,3,2,0:T(2,128)(2,1)S(1)} %copy.286) | copy-start | bytes 6148
  76.2 21.0 %copy-start.25 = (bf16[4,32,8,1,1]{1,4,3,2,0:T(2,128)(2,1)}, bf16[4,32,8,1,1]{1,4,3,2,0:T(2,128)(2,1)S(1)}, u32[]{:S(2)}) copy-start(bf16[4,32,8,1,1]{1,4,3,2,0:T(2,128)(2,1)S(1)} %copy.293) | copy-start | bytes 6148
  94.3 3.0 %copy-start.27 = (bf16[4,32,1,1,8]{1,4,3,2,0:T(8,128)(2,1)S(1)}, bf16[4,32,1,1,8]{1,4,3,2,0:T(8,128)(2,1)}, u32[]{:S(2)}) copy-start(bf16[4,32,1,1,8]{1,4,3,2,0:T(8,128)(2,1)} %slice_bitcast_fusion.40) | copy-start | bytes 6148
  94.3 3.0 %copy-start.28 = (bf16[4,32,1,1,8]{1,4,3,2,0:T(8,128)(2,1)S(1)}, bf16[4,32,1,1,8]{1,4,3,2,0:T(8,128)(2,1)}, u32[]{:S(2)}) copy-start(bf16[4,32,1,1,8]{1,4,3,2,0:T(8,128)(2,1)} %slice_bitcast_fusion.39) | copy-start | bytes 6148
  94.3 3.0 %copy-start.30 = (bf16[4,32,1,1,1]{1,4,3,2,0:T(2,128)(2,1)S(1)}, bf16[4,32,1,1,1]{1,4,3,2,0:T(2,128)(2,1)}, u32[]{:S(2)}) copy-start(bf16[4,32,1,1,1]{1,4,3,2,0:T(2,128)(2,1)} %broadcast_in_dim.250) | copy-start | bytes 772
  94.3 3.0 %copy-start.31 = (bf16[4,32,1,1,1]{1,4,3,2,0:T(2,128)(2,1)S(1)}, bf16[4,32,1,1,1]{1,4,3,2,0:T(2,128)(2,1)}, u32[]{:S(2)}) copy-start(bf16[4,32,1,1,1]{1,4,3,2,0:T(2,128)(2,1)} %broadcast_in_dim.252) | copy-start | bytes 772
  94.3 3.0 %copy-start.32 = (bf16[4,32,1,1,1]{1,4,3,2,0:T(2,128)(2,1)S(1)}, bf16[4,32,1,1,1]{1,4,3,2,0:T(2,128)(2,1)}, u32[]{:S(2)}) copy-start(bf16[4,32,1,1,1]{1,4,3,2,0:T(2,128)(2,1)} %broadcast_in_dim.251) | copy-start | bytes 772
  94.3 3.0 %copy-start.33 = (bf16[4,32,1,1,1]{1,4,3,2,0:T(2,128)(2,1)S(1)}, bf16[4,32,1,1,1]{1,4,3,2,0:T(2,128)(2,1)}, u32[]{:S(2)}) copy-start(bf16[4,32,1,1,1]{1,4,3,2,0:T(2,128)(2,1)} %broadcast_in_dim.253) | copy-start | bytes 772
  114.3 6.4 %copy-start.2 = (bf16[4,32,512]{2,1,0:T(8,128)(2,1)S(1)}, bf16[4,32,512]{2,1,0:T(8,128)(2,1)}, u32[]{:S(2)}) copy-start(bf16[4,32,512]{2,1,0:T(8,128)(2,1)} %param.9) | copy-start | bytes 393220
  142.0 3.7 %copy-start.5 = (bf16[4,32,512]{2,1,0:T(8,128)(2,1)S(1)}, bf16[4,32,512]{2,1,0:T(8,128)(2,1)}, u32[]{:S(2)}) copy-start(bf16[4,32,512]{2,1,0:T(8,128)(2,1)} %copy.321) | copy-start | bytes 393220
  142.0 3.8 %copy-start.7 = (bf16[4,32,512]{2,1,0:T(8,128)(2,1)S(1)}, bf16[4,32,512]{2,1,0:T(8,128)(2,1)}, u32[]{:S(2)}) copy-start(bf16[4,32,512]{2,1,0:T(8,128)(2,1)} %copy.322) | copy-start | bytes 393220
  142.0 3.8 %copy-start.6 = (bf16[4,32,512]{2,1,0:T(8,128)(2,1)S(1)}, bf16[4,32,512]{2,1,0:T(8,128)(2,1)}, u32[]{:S(2)}) copy-start(bf16[4,32,512]{2,1,0:T(8,128)(2,1)} %copy.332) | copy-start | bytes 393220
  142.8 3.6 %copy-start.18 = (bf16[4,32,512]{2,1,0:T(8,128)(2,1)S(1)}, bf16[4,32,512]{2,1,0:T(8,128)(2,1)}, u32[]{:S(2)}) copy-start(bf16[4,32,512]{2,1,0:T(8,128)(2,1)} %copy.333) | copy-start | bytes 393220
  142.8 4.3 %copy-start.16 = (bf16[4,32,512]{2,1,0:T(8,128)(2,1)S(1)}, bf16[4,32,512]{2,1,0:T(8,128)(2,1)}, u32[]{:S(2)}) copy-start(bf16[4,32,512]{2,1,0:T(8,128)(2,1)} %copy.334) | copy-start | bytes 393220
  142.8 5.0 %copy-start.14 = (bf16[4,32,512]{2,1,0:T(8,128)(2,1)S(1)}, bf16[4,32,512]{2,1,0:T(8,128)(2,1)}, u32[]{:S(2)}) copy-start(bf16[4,32,512]{2,1,0:T(8,128)(2,1)} %copy.335) | copy-start | bytes 393220
  142.8 5.6 %copy-start.17 = (bf16[4,32,512]{2,1,0:T(8,128)(2,1)S(1)}, bf16[4,32,512]{2,1,0:T(8,128)(2,1)}, u32[]{:S(2)}) copy-start(bf16[4,32,512]{2,1,0:T(8,128)(2,1)} %copy.323) | copy-start | bytes 393220
  142.8 5.6 %copy-start.15 = (bf16[4,32,512]{2,1,0:T(8,128)(2,1)S(1)}, bf16[4,32,512]{2,1,0:T(8,128)(2,1)}, u32[]{:S(2)}) copy-start(bf16[4,32,512]{2,1,0:T(8,128)(2,1)} %copy.324) | copy-start | bytes 393220
  142.8 5.7 %copy-start.13 = (bf16[4,32,512]{2,1,0:T(8,128)(2,1)S(1)}, bf16[4,32,512]{2,1,0:T(8,128)(2,1)}, u32[]{:S(2)}) copy-start(bf16[4,32,512]{2,1,0:T(8,128)(2,1)} %copy.325) | copy-start | bytes 393220
  143.8 4.7 %copy-start.22 = (bf16[32,9,32]{0,2,1:T(8,128)(2,1)S(1)}, bf16[32,9,32]{0,2,1:T(8,128)(2,1)}, u32[]{:S(2)}) copy-start(bf16[32,9,32]{0,2,1:T(8,128)(2,1)} %copy.326) | copy-start | bytes 55300
  (13 other events, 27.2 us)
Sparse Core Ops, SparseCore 0:
  153.3 89.8 all-reduce.4
where the time goes:
time: 254 us; the launch traced here: 252 us
  local copies, waits for them, and re-layouts  107 us (42%)
  waiting for transfers between devices  87.4 us (34%)
  blocking collectives  17.5 us (7%)
  between operations  16.4 us (6%)
  other arithmetic  13.6 us (5%)
  matrix products  5.92 us (2%)
  starting transfers between devices  4.28 us (2%)
    psum x1, waiting for transfers between devices, on_device(): totals = lax.psum(weight_grads, ('brick', 'split', 'sub'))  87.3 us
    reshape x26, local copies, waits for them, and re-layouts, contract(): padded[:, :, 1 - a:9 - a, 1 - b:9 - b, 1 - c:9 - c]  34.4 us
    unnamed x132, local copies, waits for them, and re-layouts  21.5 us
    gather x18, local copies, waits for them, and re-layouts, on_device(): jnp.take(layer_tables[c], slot_index, axis=0)  10.3 us
    concatenate x2, other arithmetic, assemble(): return jnp.concatenate(planes, axis=2)  6.94 us
    slice x4, local copies, waits for them, and re-layouts, contract(): padded[:, :, 1 - a:9 - a, 1 - b:9 - b, 1 - c:9 - c]  6.8 us
    slice x22, local copies, waits for them, and re-layouts, on_device(): pieces[a, b, c] = layer_rows[:, :, window(a), window(b)][:, :, :, :, None]  6.71 us
    broadcast_in_dim x16, local copies, waits for them, and re-layouts, on_device(): pieces[a, b, c] = layer_rows[:, :, window(a), window(b)][:, :, :, :, None]  6.67 us
  transfers between devices with their start and end apart: 3, of which 1 were waited for; matrix products, arithmetic and copies ran while one was open for 15% of the time, Pallas kernels for 0%

commit v1 on v0

--- a/solution.py
+++ b/solution.py
@@ -110,7 +110,7 @@
     grad_features = jnp.where(live_mask, input_grad, jnp.zeros_like(input_grad)).astype(
         jnp.bfloat16
     )
-    totals = lax.psum(weight_grads, ("brick", "split", "sub"))
+    totals = jnp.sum(lax.all_gather(weight_grads, ("brick", "split", "sub")), axis=0)
     scaling = 1.0 / math.sqrt(
         lax.axis_size("brick") * lax.axis_size("split") * lax.axis_size("sub") * blocks_here * 512
     )

time: 254 us -> 217 us (0.85)
  waiting for transfers between devices: 87.4 us -> 55.6 us
  local copies, waits for them, and re-layouts: 107 us -> 100 us
  other arithmetic: 13.6 us -> 16.7 us
    psum x1 -> x0, waiting for transfers between devices: 87.3 us -> none  [on_device(): totals = lax.psum(weight_grads, ('brick', 'split', 'sub'))]
    all_gather x0 -> x1, waiting for transfers between devices: none -> 55.6 us  [on_device(): lax.all_gather(weight_grads, ('brick', 'split', 'sub'))]
    unnamed x132 -> x133, local copies, waits for them, and re-layouts: 21.5 us -> 16.1 us
    reduce_sum x0 -> x1, other arithmetic: none -> 3.94 us  [on_device(): jnp.sum(lax.all_gather(weight_grads, ('brick', 'split', 'sub')), axis=0)]
  transfers between devices with their start and end apart: 3 -> 3, of which waited for: 1 -> 1; matrix products, arithmetic and copies ran while one was open for 15% -> 17% of each run, Pallas kernels for 0% -> 0%
where the time goes in v1:
time: 217 us; the launch traced here: 215 us
  local copies, waits for them, and re-layouts  100 us (46%)
  waiting for transfers between devices  55.6 us (26%)
  blocking collectives  17.5 us (8%)
  other arithmetic  16.7 us (8%)
  between operations  16.3 us (8%)
  matrix products  4.62 us (2%)
  starting transfers between devices  4.28 us (2%)
    all_gather x1, waiting for transfers between devices, on_device(): lax.all_gather(weight_grads, ('brick', 'split', 'sub'))  55.6 us
    reshape x26, local copies, waits for them, and re-layouts, contract(): padded[:, :, 1 - a:9 - a, 1 - b:9 - b, 1 - c:9 - c]  34.1 us
    unnamed x133, local copies, waits for them, and re-layouts  16.1 us
    gather x18, local copies, waits for them, and re-layouts, on_device(): jnp.take(layer_tables[c], slot_index, axis=0)  10.3 us
    concatenate x2, other arithmetic, assemble(): return jnp.concatenate(planes, axis=2)  7.2 us
    slice x4, local copies, waits for them, and re-layouts, contract(): padded[:, :, 1 - a:9 - a, 1 - b:9 - b, 1 - c:9 - c]  7.04 us
    slice x22, local copies, waits for them, and re-layouts, on_device(): pieces[a, b, c] = layer_rows[:, :, window(a), window(b)][:, :, :, :, None]  6.71 us
    all_gather x1, blocking collectives, on_device(): lax.all_gather(upper_layer, ('split', 'sub'), axis=0, tiled=True)  6.18 us
  transfers between devices with their start and end apart: 3, of which 1 were waited for; matrix products, arithmetic and copies ran while one was open for 17% of the time, Pallas kernels for 0%

profile of v1, /device:TPU:0, one launch (start us, length us, event | category | flops | bytes accessed | tf_op | source)
XLA Modules:
  0.0 215.3 jit_solution(11784762677861618131)
XLA Ops:
  9.1 6.2 %all-gather.1 = bf16[4,4,2048]{2,1,0:T(4,128)(2,1)S(1)} all-gather(bf16[1,4,2048]{2,1,0:T(4,128)(2,1)S(1)} %reshape.485), channel_id=1, replica_groups=mesh['groups'=2,'brick'=4,'split'=2,'sub'=2] {'split','sub'}, dimensions={0}, use_global_device_ids=true | all-gather | bytes 81920 | tf_op jit(solution)/shard_map/all_gather | solution.py:82
  15.3 2.2 collective-permute-start
  18.0 5.2 %all-gather.2 = bf16[4,4,2048]{2,1,0:T(4,128)(2,1)S(1)} all-gather(bf16[1,4,2048]{2,1,0:T(4,128)(2,1)S(1)} %reshape.487), channel_id=1, replica_groups=mesh['groups'=2,'brick'=4,'split'=2,'sub'=2] {'split','sub'}, dimensions={0}, use_global_device_ids=true | all-gather | bytes 81920 | tf_op jit(solution)/shard_map/all_gather | solution.py:81
  23.2 2.1 collective-permute-start.1
  27.7 6.1 %all_gather.16 = bf16[16,32,256]{2,1,0:T(8,128)(2,1)S(1)} all-gather(bf16[4,32,256]{2,1,0:T(8,128)(2,1)S(1)} %copy.280), channel_id=1, replica_groups=mesh['groups'=2,'brick'=4,'split'=2,'sub'=2] {'split','sub'}, dimensions={0}, use_global_device_ids=true | all-gather | bytes 327680 | tf_op jit(solution)/shard_map/all_gather | solution.py:80
  78.1 1.7 maximum_maximum_fusion.3
  81.2 1.9 copy.343
  83.1 1.9 copy.331
  86.9 1.9 copy.341
  89.9 3.7 %maximum_maximum_fusion = bf16[4,32,9,10,10]{1,4,3,2,0:T(8,128)(2,1)S(1)} fusion(bf16[4,32,1,1,1]{1,4,3,2,0:T(2,128)(2,1)S(1)} %copy-done.33, bf16[4,32,1,1,8]{1,4,3,2,0:T(8,128)(2,1)S(1)} %copy-done.28, bf16[4,32,1,1,1]{1,4,3,2,0:T(2,128)(2,1)S(1)} %copy-done.31, bf16[4,32,1,8,1]{1,4,3,2,0:T(2,128)(2,1)S(1)} %copy.300, ...), kind=kLoop, calls=%fused_computation.26 | loop fusion | flops 4147200 | bytes 460800 | tf_op jit(solution)/shard_map/concatenate | solution.py:32
  93.5 2.3 %fusion.7 = (bf16[4,32,8,8,8]{1,4,3,2,0:T(8,128)(2,1)}, bf16[4,32,8,8,8]{1,4,3,2,0:T(8,128)(2,1)}, bf16[4,32,8,8,8]{1,4,3,2,0:T(8,128)(2,1)}, bf16[4,32,8,8,8]{1...) fusion(bf16[4,32,9,10,10]{1,4,3,2,0:T(8,128)(2,1)S(1)} %maximum, ...), kind=kLoop, calls=%fused_computation.305 | loop fusion | bytes 2359296 | tf_op jit(solution)/shard_map/slice | solution.py:42
  95.8 1.9 copy.340
  97.7 1.9 copy.339
  107.1 3.5 %maximum_maximum_fusion.1 = bf16[4,32,9,10,10]{1,4,3,2,0:T(8,128)(2,1)S(1)} fusion(bf16[4,32,8,1,1]{1,4,3,2,0:T(2,128)(2,1)} %copy-done.26, bf16[4,32,8,1,8]{1,4,3,2,0:T(8,128)(2,1)S(1)} %slice_bitcast_fusion.4, bf16[4,32,8,1,1]{1,4,3,2,0:T(2,128)(2,1)} %copy-done.24, bf16[4,32,8,8,1]{1,4,3,2,0:T(2,128)(2,1)S(1)} %copy.287, ...), kind=kLoop, calls=%fused_computation.27 | loop fusion | flops 4147200 | bytes 460800 | tf_op jit(solution)/shard_map/concatenate | solution.py:32
  110.6 2.4 %fusion.6 = (bf16[4,32,8,8,8]{1,4,3,2,0:T(8,128)(2,1)}, bf16[4,32,8,8,8]{1,4,3,2,0:T(8,128)(2,1)}, bf16[4,32,8,8,8]{1,4,3,2,0:T(8,128)(2,1)}, bf16[4,32,8,8,8]{1...) fusion(bf16[4,32,9,10,10]{1,4,3,2,0:T(8,128)(2,1)S(1)} %maximum, ...), kind=kLoop, calls=%fused_computation.304 | loop fusion | bytes 2359296 | tf_op jit(solution)/shard_map/slice | solution.py:42
  113.0 1.9 copy.346
  114.9 1.9 copy.345
  116.7 1.9 copy.344
  118.6 1.9 copy.334
  120.5 1.9 copy.333
  122.4 1.9 copy.332
  124.2 1.9 copy.324
  147.7 55.6 %all-gather.5.cloned.1.call-done = f32[432,32,32]{2,1,0:T(8,128)} async-done(((f32[27,32,32]{2,1,0:T(8,128)}), f32[432,32,32]{2,1,0:T(8,128)}) %all-gather.5.cloned.1.call-update) | async-done | bytes 1769488 | tf_op jit(solution)/shard_map/all_gather | solution.py:113
  203.3 3.9 %reduce_sum.9 = f32[27,32,32]{2,1,0:T(8,128)S(1)} reduce(f32[16,27,32,32]{3,2,1,0:T(8,128)} %bitcast.237, f32[]{:T(128)} %constant.20.clone.1), dimensions={0}, to_apply=%region_0.3 | reduce | flops 414720 | bytes 1880068 | tf_op jit(solution)/shard_map/reduce_sum | solution.py:113
  (367 shorter events, 81.5 us)
Async XLA Ops:
  7.2 18.1 %copy-start.3 = (s32[4,26]{1,0:T(4,128)S(1)}, s32[4,26]{1,0:T(4,128)}, u32[]{:S(2)}) copy-start(s32[4,26]{1,0:T(4,128)} %param.13) | copy-start | bytes 1252
  7.2 196.1 %all-gather.5.cloned.1.call-start = ((), (), s32[]{:S(2)}) async-start(), calls=%async_computation | async-start | bytes 7520256 | tf_op jit(solution)/shard_map/all_gather | solution.py:113
  15.3 28.8 %collective-permute-start = (bf16[16,2048]{1,0:T(8,128)(2,1)S(1)}, bf16[16,2048]{1,0:T(8,128)(2,1)S(1)}, u32[]{:S(2)}, u32[]{:S(2)}) collective-permute-start(bf16[16,2048]{1,0:T(8,128)(2,1)S(1)} %reshape.486), channel_id=1, source_target_pairs={{12,0},{0,4},{4,8},{8,12},{13,1},{1,5},{5,9},{9,13},{14,2},{2,6},{... | collective-permute-start | bytes 196616 | tf_op jit(solution)/shard_map/ppermute | solution.py:14
  23.2 36.6 %collective-permute-start.1 = (bf16[16,2048]{1,0:T(8,128)(2,1)S(1)}, bf16[16,2048]{1,0:T(8,128)(2,1)S(1)}, u32[]{:S(2)}, u32[]{:S(2)}) collective-permute-start(bf16[16,2048]{1,0:T(8,128)(2,1)S(1)} %reshape.488), channel_id=1, source_target_pairs={{4,0},{8,4},{12,8},{0,12},{5,1},{9,5},{13,9},{1,13},{6,2},{10,6},{... | collective-permute-start | bytes 196616 | tf_op jit(solution)/shard_map/ppermute | solution.py:14
  51.6 38.2 %copy-start.24 = (bf16[4,32,8,1,1]{1,4,3,2,0:T(2,128)(2,1)}, bf16[4,32,8,1,1]{1,4,3,2,0:T(2,128)(2,1)S(1)}, u32[]{:S(2)}) copy-start(bf16[4,32,8,1,1]{1,4,3,2,0:T(2,128)(2,1)S(1)} %copy.291) | copy-start | bytes 6148
  66.6 23.2 %copy-start.25 = (bf16[4,32,8,1,1]{1,4,3,2,0:T(2,128)(2,1)}, bf16[4,32,8,1,1]{1,4,3,2,0:T(2,128)(2,1)S(1)}, u32[]{:S(2)}) copy-start(bf16[4,32,8,1,1]{1,4,3,2,0:T(2,128)(2,1)S(1)} %copy.285) | copy-start | bytes 6148
  67.4 22.4 %copy-start.26 = (bf16[4,32,8,1,1]{1,4,3,2,0:T(2,128)(2,1)}, bf16[4,32,8,1,1]{1,4,3,2,0:T(2,128)(2,1)S(1)}, u32[]{:S(2)}) copy-start(bf16[4,32,8,1,1]{1,4,3,2,0:T(2,128)(2,1)S(1)} %copy.292) | copy-start | bytes 6148
  81.2 3.8 %copy-start.2 = (bf16[4,32,8,8,8]{1,4,3,2,0:T(8,128)(2,1)S(1)}, bf16[4,32,8,8,8]{1,4,3,2,0:T(8,128)(2,1)}, u32[]{:S(2)}) copy-start(bf16[4,32,8,8,8]{1,4,3,2,0:T(8,128)(2,1)} %get-tuple-element.54) | copy-start | bytes 393220
  86.9 3.0 %copy-start.28 = (bf16[4,32,1,1,8]{1,4,3,2,0:T(8,128)(2,1)S(1)}, bf16[4,32,1,1,8]{1,4,3,2,0:T(8,128)(2,1)}, u32[]{:S(2)}) copy-start(bf16[4,32,1,1,8]{1,4,3,2,0:T(8,128)(2,1)} %slice_bitcast_fusion.39) | copy-start | bytes 6148
  86.9 3.0 %copy-start.30 = (bf16[4,32,1,1,1]{1,4,3,2,0:T(2,128)(2,1)S(1)}, bf16[4,32,1,1,1]{1,4,3,2,0:T(2,128)(2,1)}, u32[]{:S(2)}) copy-start(bf16[4,32,1,1,1]{1,4,3,2,0:T(2,128)(2,1)} %broadcast_in_dim.250) | copy-start | bytes 772
  86.9 3.0 %copy-start.31 = (bf16[4,32,1,1,1]{1,4,3,2,0:T(2,128)(2,1)S(1)}, bf16[4,32,1,1,1]{1,4,3,2,0:T(2,128)(2,1)}, u32[]{:S(2)}) copy-start(bf16[4,32,1,1,1]{1,4,3,2,0:T(2,128)(2,1)} %broadcast_in_dim.252) | copy-start | bytes 772
  86.9 3.0 %copy-start.32 = (bf16[4,32,1,1,1]{1,4,3,2,0:T(2,128)(2,1)S(1)}, bf16[4,32,1,1,1]{1,4,3,2,0:T(2,128)(2,1)}, u32[]{:S(2)}) copy-start(bf16[4,32,1,1,1]{1,4,3,2,0:T(2,128)(2,1)} %broadcast_in_dim.251) | copy-start | bytes 772
  86.9 3.0 %copy-start.33 = (bf16[4,32,1,1,1]{1,4,3,2,0:T(2,128)(2,1)S(1)}, bf16[4,32,1,1,1]{1,4,3,2,0:T(2,128)(2,1)}, u32[]{:S(2)}) copy-start(bf16[4,32,1,1,1]{1,4,3,2,0:T(2,128)(2,1)} %broadcast_in_dim.253) | copy-start | bytes 772
  124.2 6.5 %copy-start.9 = (bf16[4,32,512]{2,1,0:T(8,128)(2,1)S(1)}, bf16[4,32,512]{2,1,0:T(8,128)(2,1)}, u32[]{:S(2)}) copy-start(bf16[4,32,512]{2,1,0:T(8,128)(2,1)} %copy.320) | copy-start | bytes 393220
  127.0 3.8 %copy-start.11 = (bf16[4,32,512]{2,1,0:T(8,128)(2,1)S(1)}, bf16[4,32,512]{2,1,0:T(8,128)(2,1)}, u32[]{:S(2)}) copy-start(bf16[4,32,512]{2,1,0:T(8,128)(2,1)} %copy.321) | copy-start | bytes 393220
  127.0 3.8 %copy-start.10 = (bf16[4,32,512]{2,1,0:T(8,128)(2,1)S(1)}, bf16[4,32,512]{2,1,0:T(8,128)(2,1)}, u32[]{:S(2)}) copy-start(bf16[4,32,512]{2,1,0:T(8,128)(2,1)} %copy.331) | copy-start | bytes 393220
  127.0 5.1 %copy-start.20 = (bf16[4,32,512]{2,1,0:T(8,128)(2,1)S(1)}, bf16[4,32,512]{2,1,0:T(8,128)(2,1)}, u32[]{:S(2)}) copy-start(bf16[4,32,512]{2,1,0:T(8,128)(2,1)} %copy.333) | copy-start | bytes 393220
  127.0 5.8 %copy-start.18 = (bf16[4,32,512]{2,1,0:T(8,128)(2,1)S(1)}, bf16[4,32,512]{2,1,0:T(8,128)(2,1)}, u32[]{:S(2)}) copy-start(bf16[4,32,512]{2,1,0:T(8,128)(2,1)} %copy.334) | copy-start | bytes 393220
  127.8 3.6 %copy-start.22 = (bf16[4,32,512]{2,1,0:T(8,128)(2,1)S(1)}, bf16[4,32,512]{2,1,0:T(8,128)(2,1)}, u32[]{:S(2)}) copy-start(bf16[4,32,512]{2,1,0:T(8,128)(2,1)} %copy.332) | copy-start | bytes 393220
  127.8 5.6 %copy-start.21 = (bf16[4,32,512]{2,1,0:T(8,128)(2,1)S(1)}, bf16[4,32,512]{2,1,0:T(8,128)(2,1)}, u32[]{:S(2)}) copy-start(bf16[4,32,512]{2,1,0:T(8,128)(2,1)} %copy.322) | copy-start | bytes 393220
  127.8 5.6 %copy-start.19 = (bf16[4,32,512]{2,1,0:T(8,128)(2,1)S(1)}, bf16[4,32,512]{2,1,0:T(8,128)(2,1)}, u32[]{:S(2)}) copy-start(bf16[4,32,512]{2,1,0:T(8,128)(2,1)} %copy.323) | copy-start | bytes 393220
  127.8 5.6 %copy-start.17 = (bf16[4,32,512]{2,1,0:T(8,128)(2,1)S(1)}, bf16[4,32,512]{2,1,0:T(8,128)(2,1)}, u32[]{:S(2)}) copy-start(bf16[4,32,512]{2,1,0:T(8,128)(2,1)} %copy.324) | copy-start | bytes 393220
  128.8 4.7 %copy-start.4 = (bf16[4,32,512]{2,1,0:T(8,128)(2,1)S(1)}, bf16[4,32,512]{2,1,0:T(8,128)(2,1)}, u32[]{:S(2)}) copy-start(bf16[4,32,512]{2,1,0:T(8,128)(2,1)} %param.10) | copy-start | bytes 393220
  128.8 4.7 %copy-start.29 = (pred[4]{0:T(512)(128)(4,1)S(1)}, pred[4]{0:T(512)(128)(4,1)}, u32[]{:S(2)}) copy-start(pred[4]{0:T(512)(128)(4,1)} %iota_compare_fusion) | copy-start | bytes 16
  (13 other events, 18.6 us)
Sparse Core Ops, SparseCore 0:
  137.7 65.5 all-gather.4
